TPU v7x, 32 devices: a whole 2x2x4 slice. The times are simulated.
32 devices in a mesh: grp: 4 (over x, core), ep: 8 (over z, y).
Axes of the slice: x: 2, y: 2, z: 4, core: 2. Of those that a mesh axis runs over, the one named last changes fastest.
Arguments:
- tokens: bfloat16 [2048, 5120], P('ep', 'grp'), may hold values from -6 to 6
- cotangent: bfloat16 [2048, 5120], P('ep', 'grp'), may hold values from -0.59765625 to 0.59765625
- gate_weights: bfloat16 [2048, 6], P('ep'), may hold values from 0.099609375 to 1
- expert_ids: int32 [2048, 6], P('ep'), may hold values from 0 to 159, all different within a row; in each aligned block of 256 rows (0 to 255, 256 to 511, ...) at most 16 rows name the same one
- hot_ids: int32 [2], replicated, may hold values from 8 to 159, as said below
- gate_cold: bfloat16 [8, 5120, 768], P('ep', 'grp'), may hold values from -0.078125 to 0.078125
- up_cold: bfloat16 [8, 5120, 768], P('ep', 'grp'), may hold values from -0.078125 to 0.078125
- down_cold: bfloat16 [8, 768, 5120], P('ep', None, 'grp'), may hold values from -0.21875 to 0.21875
- gate_hot: bfloat16 [2, 5120, 768], P(None, 'grp', 'ep'), may hold values from -0.078125 to 0.078125
- up_hot: bfloat16 [2, 5120, 768], P(None, 'grp', 'ep'), may hold values from -0.078125 to 0.078125
- down_hot: bfloat16 [2, 768, 5120], P(None, 'ep', 'grp'), may hold values from -0.21875 to 0.21875
Outputs:
- grad_gate_cold: bfloat16 [8, 5120, 768], P('ep', 'grp')
- grad_up_cold: bfloat16 [8, 5120, 768], P('ep', 'grp')
- grad_down_cold: bfloat16 [8, 768, 5120], P('ep', None, 'grp')
- grad_gate_hot: float32 [2, 5120, 768], P(None, 'grp', 'ep')
- grad_up_hot: float32 [2, 5120, 768], P(None, 'grp', 'ep')
- grad_down_hot: float32 [2, 768, 5120], P(None, 'ep', 'grp')
- gate_weight_grad: float32 [2048, 6], P('ep')
Inputs may be any that keep to these rules, and one draw needn't show every extreme that they name: `expert_ids`: each row names 6 different experts. Among the routes of the 256 tokens of one index of ep (aligned blocks of rows) no expert is named more than 16 times, a bound that some block reaches. `hot_ids`: distinct expert numbers, none below 8; expert 160 - 1 is always among them.
All inputs are finite; a program needn't handle non-finite values.
Results may differ from a plain program's by a relative error of at most 0.02.
Values may be sent and summed in bfloat16 or wider, within the bound.
No kernel may reach another device: no remote copies, remote signals or barrier semaphores. Data moves between devices by JAX's collectives and lax.ppermute only.
A program may use at most 128 MiB of HBM per device.

v0:
```python
import jax
import jax.numpy as jnp
from jax import lax
from jax.sharding import PartitionSpec as P


def route_table(flat_ids, targets, capacity):
    matches = (flat_ids[:, None] == targets[None, :]).astype(jnp.int32)
    rank_of = jnp.cumsum(matches, axis=0) - 1
    slot_of = jnp.sum(matches * rank_of, axis=1)
    owner_of = jnp.sum(matches * jnp.arange(targets.shape[0], dtype=jnp.int32)[None, :], axis=1)
    usable = jnp.sum(matches, axis=1) > 0
    row_of = owner_of * capacity + slot_of
    rows_total = targets.shape[0] * capacity
    route_map = (row_of[None, :] == jnp.arange(rows_total, dtype=jnp.int32)[:, None]) & usable[
        None, :
    ]
    return route_map.astype(jnp.float32)


def gather_rows(route_map, tokens, cotangent, flat_weights, tok_rows, top_count):
    per_token = jnp.sum(route_map.reshape(route_map.shape[0], tok_rows, top_count), axis=2)
    token_map = per_token.astype(jnp.bfloat16)
    feat_rows = jnp.dot(token_map, tokens, preferred_element_type=jnp.float32).astype(jnp.bfloat16)
    cotan_rows = jnp.dot(token_map, cotangent, preferred_element_type=jnp.float32).astype(
        jnp.bfloat16
    )
    scale_rows = jnp.dot(
        route_map, flat_weights.astype(jnp.float32), precision=lax.Precision.HIGHEST
    )
    return (feat_rows, cotan_rows, scale_rows.astype(jnp.bfloat16))


def swiglu_back(pre_gate, pre_up, grad_hidden):
    sigmoid_gate = jax.nn.sigmoid(pre_gate)
    activated = pre_gate * sigmoid_gate
    hidden = (activated * pre_up).astype(jnp.bfloat16)
    back_gate = (
        grad_hidden * pre_up * sigmoid_gate * (1.0 + pre_gate * (1.0 - sigmoid_gate))
    ).astype(jnp.bfloat16)
    back_up = (grad_hidden * activated).astype(jnp.bfloat16)
    return (hidden, back_gate, back_up)


def body(
    tokens,
    cotangent,
    gate_weights,
    expert_ids,
    hot_ids,
    gate_cold,
    up_cold,
    down_cold,
    gate_hot,
    up_hot,
    down_hot,
):
    tok_rows, slice_width = tokens.shape
    top_count = expert_ids.shape[1]
    cold_count = lax.axis_size("ep")
    hot_count = hot_ids.shape[0]
    capacity = tok_rows // 16
    flat_ids = expert_ids.reshape(-1)
    flat_weights = gate_weights.reshape(-1)
    cold_map = route_table(flat_ids, jnp.arange(cold_count, dtype=jnp.int32), capacity)
    hot_map = route_table(flat_ids, hot_ids, capacity)
    cold_feats, cold_cotan, cold_scale = gather_rows(
        cold_map, tokens, cotangent, flat_weights, tok_rows, top_count
    )
    hot_feats, hot_cotan, hot_scale = gather_rows(
        hot_map, tokens, cotangent, flat_weights, tok_rows, top_count
    )
    outgoing = (
        cold_feats.reshape(cold_count, capacity, slice_width),
        cold_cotan.reshape(cold_count, capacity, slice_width),
        cold_scale.reshape(cold_count, capacity),
    )
    recv_feats, recv_cotan, recv_scale = (
        lax.all_to_all(outgoing[0], "ep", split_axis=0, concat_axis=0, tiled=True),
        lax.all_to_all(outgoing[1], "ep", split_axis=0, concat_axis=0, tiled=True),
        lax.all_to_all(outgoing[2], "ep", split_axis=0, concat_axis=0, tiled=True),
    )
    recv_feats = recv_feats.reshape(-1, slice_width)
    recv_cotan = recv_cotan.reshape(-1, slice_width)
    weighted = (
        recv_scale.reshape(-1).astype(jnp.float32)[:, None] * recv_cotan.astype(jnp.float32)
    ).astype(jnp.bfloat16)
    w_gate = gate_cold[0]
    w_up = up_cold[0]
    w_down = down_cold[0]
    part_gate = jnp.dot(recv_feats, w_gate, preferred_element_type=jnp.float32)
    part_up = jnp.dot(recv_feats, w_up, preferred_element_type=jnp.float32)
    part_hidden = lax.dot_general(
        weighted, w_down, (((1,), (1,)), ((), ())), preferred_element_type=jnp.float32
    )
    pre_gate, pre_up, grad_hidden = (
        lax.psum(part_gate.astype(jnp.bfloat16), "grp").astype(jnp.float32),
        lax.psum(part_up.astype(jnp.bfloat16), "grp").astype(jnp.float32),
        lax.psum(part_hidden.astype(jnp.bfloat16), "grp").astype(jnp.float32),
    )
    hidden, back_gate, back_up = swiglu_back(pre_gate, pre_up, grad_hidden)
    output_slice = jnp.dot(hidden, w_down, preferred_element_type=jnp.float32)
    cold_route = jnp.sum(output_slice * recv_cotan.astype(jnp.float32), axis=1)
    contract_rows = (((0,), (0,)), ((), ()))
    grad_gate_cold = lax.dot_general(
        recv_feats, back_gate, contract_rows, preferred_element_type=jnp.float32
    )
    grad_up_cold = lax.dot_general(
        recv_feats, back_up, contract_rows, preferred_element_type=jnp.float32
    )
    grad_down_cold = lax.dot_general(
        hidden, weighted, contract_rows, preferred_element_type=jnp.float32
    )
    hot_weighted_local = (
        hot_scale.astype(jnp.float32)[:, None] * hot_cotan.astype(jnp.float32)
    ).astype(jnp.bfloat16)
    blocks = lax.axis_size("ep")
    stacked = jnp.stack([hot_feats, hot_cotan, hot_weighted_local])
    all_rows = lax.all_gather(stacked, "ep", axis=1, tiled=False)
    all_rows = all_rows.reshape(3, blocks, hot_count, capacity, slice_width)
    all_rows = jnp.transpose(all_rows, (0, 2, 1, 3, 4)).reshape(
        3, hot_count, blocks * capacity, slice_width
    )
    rows_feat, rows_cot, rows_wt = (all_rows[0], all_rows[1], all_rows[2])
    part_gate_hot = jnp.einsum(
        "jrd,jdh->jrh", rows_feat, gate_hot, preferred_element_type=jnp.float32
    )
    part_up_hot = jnp.einsum("jrd,jdh->jrh", rows_feat, up_hot, preferred_element_type=jnp.float32)
    part_hidden_hot = jnp.einsum(
        "jrd,jhd->jrh", rows_wt, down_hot, preferred_element_type=jnp.float32
    )
    cot_down = jnp.einsum("jrd,jhd->jrh", rows_cot, down_hot, preferred_element_type=jnp.float32)
    hot_parts = lax.psum(
        jnp.stack([part_gate_hot, part_up_hot, part_hidden_hot]).astype(jnp.bfloat16), "grp"
    ).astype(jnp.float32)
    hidden_hot, back_gate_hot, back_up_hot = swiglu_back(hot_parts[0], hot_parts[1], hot_parts[2])
    hot_route_part = jnp.sum(hidden_hot.astype(jnp.float32) * cot_down, axis=2)
    hidden_blk = hidden_hot.shape[2]
    feat_b = rows_feat.reshape(hot_count, blocks, capacity, slice_width)
    wt_b = rows_wt.reshape(hot_count, blocks, capacity, slice_width)
    bg_b = back_gate_hot.reshape(hot_count, blocks, capacity, hidden_blk)
    bu_b = back_up_hot.reshape(hot_count, blocks, capacity, hidden_blk)
    hid_b = hidden_hot.reshape(hot_count, blocks, capacity, hidden_blk)
    blk_gate = jnp.einsum("jbcd,jbch->jbdh", feat_b, bg_b, preferred_element_type=jnp.float32)
    blk_up = jnp.einsum("jbcd,jbch->jbdh", feat_b, bu_b, preferred_element_type=jnp.float32)
    blk_down = jnp.einsum("jbch,jbcd->jbhd", hid_b, wt_b, preferred_element_type=jnp.float32)
    grad_gate_hot = jnp.sum(blk_gate.astype(jnp.bfloat16).astype(jnp.float32), axis=1)
    grad_up_hot = jnp.sum(blk_up.astype(jnp.bfloat16).astype(jnp.float32), axis=1)
    grad_down_hot = jnp.sum(blk_down.astype(jnp.bfloat16).astype(jnp.float32), axis=1)
    hot_route_all = lax.psum(hot_route_part, ("grp", "ep"))
    me = lax.axis_index("ep")
    hot_route = lax.dynamic_index_in_dim(
        hot_route_all.reshape(hot_count, blocks, capacity), me, axis=1, keepdims=False
    )
    cold_route = lax.psum(cold_route, "grp")
    cold_back = lax.all_to_all(
        cold_route.reshape(cold_count, capacity), "ep", split_axis=0, concat_axis=0, tiled=True
    )
    route_flat = jnp.dot(cold_back.reshape(-1), cold_map, precision=lax.Precision.HIGHEST)
    route_flat = route_flat + jnp.dot(
        hot_route.reshape(-1), hot_map, precision=lax.Precision.HIGHEST
    )
    gate_weight_grad = route_flat.reshape(tok_rows, top_count)
    return (
        grad_gate_cold[None].astype(jnp.bfloat16),
        grad_up_cold[None].astype(jnp.bfloat16),
        grad_down_cold[None].astype(jnp.bfloat16),
        grad_gate_hot,
        grad_up_hot,
        grad_down_hot,
        gate_weight_grad,
    )


def solution(mesh):
    in_specs = (
        P("ep", "grp"),
        P("ep", "grp"),
        P("ep", None),
        P("ep", None),
        P(),
        P("ep", "grp", None),
        P("ep", "grp", None),
        P("ep", None, "grp"),
        P(None, "grp", "ep"),
        P(None, "grp", "ep"),
        P(None, "ep", "grp"),
    )
    out_specs = (
        P("ep", "grp", None),
        P("ep", "grp", None),
        P("ep", None, "grp"),
        P(None, "grp", "ep"),
        P(None, "grp", "ep"),
        P(None, "ep", "grp"),
        P("ep", None),
    )
    return jax.shard_map(body, mesh=mesh, in_specs=in_specs, out_specs=out_specs, check_vma=False)
```

profile of v0, /device:TPU:0, one launch (start us, length us, event | category | flops | bytes accessed | tf_op | source)
XLA Modules:
  0.0 194.5 jit_solution(9976301442183095189)
XLA Ops:
  7.2 1.0 copy.45
  8.5 0.8 copy.49
  9.5 0.7 compare_convert_fusion.1
  10.2 0.6 reduce-window.16
  11.2 0.8 fusion.78
  12.8 1.3 convolution_convert_fusion.8
  14.4 0.7 pad_maximum_fusion
  15.2 2.3 %reduce-window.14 = s32[8,12,128]{2,1,0:T(8,128)S(1)} reduce-window(s32[8,12,128]{2,1,0:T(8,128)S(1)} %fusion.69, s32[]{:T(128)} %constant.15.clone.1), window={size=1x1x128 pad=0_0x0_0x127_0}, to_apply=%region_1.2 | reduce-window | flops 1560576 | bytes 98308 | tf_op jit(solution)/shard_map/reduce-window
  17.5 0.3 slice_reduce_fusion
  18.4 0.7 all_to_all.24
  19.1 7.3 %all-to-all-start.1 = ((bf16[8,1,16]{2,1,0:T(2,128)(2,1)}), bf16[8,1,16]{2,1,0:T(2,128)(2,1)S(1)}, u32[]{:S(2)}, u32[]{:S(2)}) async-start(bf16[8,1,16]{2,1,0:T(2,128)(2,1)} %all_to_all.24), calls=%async_computation.1 | async-start | bytes 8192 | tf_op jit(solution)/shard_map/all_to_all | solution.py:81
  27.0 1.0 convolution_convert_fusion.7
  28.0 4.8 %all-to-all-done.1 = bf16[8,1,16]{2,1,0:T(2,128)(2,1)S(1)} async-done(((bf16[8,1,16]{2,1,0:T(2,128)(2,1)}), bf16[8,1,16]{2,1,0:T(2,128)(2,1)S(1)}, u32[]{:S(2)}, u32[]{:S(2)}) %all-to-all-start.1) | async-done | bytes 288 | tf_op jit(solution)/shard_map/all_to_all | solution.py:81
  32.8 3.4 %all-to-all-start = ((bf16[8,16,1280]{2,1,0:T(8,128)(2,1)}), bf16[8,16,1280]{2,1,0:T(8,128)(2,1)S(1)}, u32[]{:S(2)}, u32[]{:S(2)}) async-start(bf16[8,16,1280]{2,1,0:T(8,128)(2,1)} %bitcast.165), calls=%async_computation | async-start | bytes 655360 | tf_op jit(solution)/shard_map/all_to_all | solution.py:79
  36.2 1.0 convolution_convert_fusion.6
  37.3 9.1 %all-to-all-done = bf16[8,16,1280]{2,1,0:T(8,128)(2,1)S(1)} async-done(((bf16[8,16,1280]{2,1,0:T(8,128)(2,1)}), bf16[8,16,1280]{2,1,0:T(8,128)(2,1)S(1)}, u32[]{:S(2)}, u32[]{:S(2)}) %all-to-all-start) | async-done | bytes 327712 | tf_op jit(solution)/shard_map/all_to_all | solution.py:79
  46.4 3.9 %all-to-all-start.2 = ((bf16[8,16,1280]{2,1,0:T(8,128)(2,1)}), bf16[8,16,1280]{2,1,0:T(8,128)(2,1)S(1)}, u32[]{:S(2)}, u32[]{:S(2)}) async-start(bf16[8,16,1280]{2,1,0:T(8,128)(2,1)} %bitcast.166), calls=%async_computation.2 | async-start | bytes 655360 | tf_op jit(solution)/shard_map/all_to_all | solution.py:80
  50.3 2.8 %fusion.20 = bf16[128,768]{1,0:T(8,128)(2,1)} fusion(bf16[128,1280]{1,0:T(8,128)(2,1)S(1)} %bitcast.155, bf16[1,1280,768]{2,1,0:T(8,128)(2,1)} %param.16), kind=kOutput, calls=%fused_computation.29 | convolution fusion | flops 251756544 | bytes 2490368 | tf_op jit(solution)/shard_map/dot_general | solution.py:91
  53.1 1.1 fusion.17
  54.3 14.6 %all-to-all-done.2 = bf16[8,16,1280]{2,1,0:T(8,128)(2,1)S(1)} async-done(((bf16[8,16,1280]{2,1,0:T(8,128)(2,1)}), bf16[8,16,1280]{2,1,0:T(8,128)(2,1)S(1)}, u32[]{:S(2)}, u32[]{:S(2)}) %all-to-all-start.2) | async-done | bytes 327712 | tf_op jit(solution)/shard_map/all_to_all | solution.py:80
  69.0 1.5 fusion.14
  70.5 2.1 %all-gather.3.cloned.1.call-done = bf16[3,256,1280]{2,1,0:T(8,128)(2,1)} async-done(((bf16[3,32,1280]{2,1,0:T(8,128)(2,1)}), bf16[3,256,1280]{2,1,0:T(8,128)(2,1)}) %all-gather.3.cloned.1.call-update) | async-done | bytes 1966096 | tf_op jit(solution)/shard_map/all_gather | solution.py:119
  72.6 1.7 copy.68
  74.4 1.0 fusion.92
  75.3 0.5 copy-done.1
  75.8 0.3 fusion.25
  76.3 0.3 fusion.24
  76.6 0.3 copy-done.10
  76.9 0.3 fusion.26
  77.2 0.7 pad_maximum_fusion.1
  78.1 33.6 %all-reduce.3.cloned.1.call-done = (bf16[128,768]{1,0:T(8,128)(2,1)}, bf16[128,768]{1,0:T(8,128)(2,1)}, bf16[128,768]{1,0:T(8,128)(2,1)}, bf16[3,2,128,96]{2,3,1,0:T(8,128)(2,1)}) async-done(((bf16[128,768]{1,0:T(8,128)(2,1)}, bf16[128,768]{1,0:T(8,128)(2,1)}, bf16[128,768]{1,0:T(8,128)(2,1)}, bf16[3,2,128,96]{2,3,1,0:T(8,128)(2,1)}), (bf16[128,768]{1,0:T(8,128)(2,1)}, bf16[128,768]{1,0:T(8,128)(2,1)}, ...) | async-done | bytes 737296 | tf_op jit(solution)/shard_map/psum | solution.py:98
  111.7 1.6 convert_element_type.217
  113.3 0.9 fusion.93
  114.5 3.3 %convert_reduce_fusion = f32[2,96,1280]{2,1,0:T(8,128)} fusion(f32[2,8,16,96]{3,2,1,0:T(8,128)S(1)} %bitcast.169, f32[2,8,16,96]{3,2,1,0:T(8,128)S(1)} %bitcast.171, bf16[3,2,8,16,1280]{4,3,2,1,0:T(8,128)(2,1)} %bitcast.152), kind=kOutput, calls=%fused_computation | convolution fusion | flops 68714496 | bytes 1835008 | tf_op jit(solution)/shard_map/jbch,jbcd->jbhd/dot_general | solution.py:146
  117.8 3.3 %convert_reduce_fusion.2 = f32[2,1280,96]{1,2,0:T(8,128)} fusion(f32[2,8,16,96]{3,2,1,0:T(8,128)S(1)} %bitcast.172, f32[2,8,16,96]{3,2,1,0:T(8,128)S(1)} %bitcast.174, f32[2,8,16,96]{3,2,1,0:T(8,128)S(1)} %bitcast.170, bf16[3,2,8,16,1280]{4,3,2,1,0:T(8,128)(2,1)} %bitcast.153), kind=kOutput, calls=%fused_computation.2 | convolution fusion | flops 68812800 | bytes 1933312 | tf_op jit(solution)/shard_map/jbcd,jbch->jbdh/dot_general | solution.py:144
  121.1 3.4 %convert_reduce_fusion.1 = f32[2,1280,96]{1,2,0:T(8,128)} fusion(f32[2,8,16,96]{3,2,1,0:T(8,128)S(1)} %bitcast.175, f32[2,8,16,96]{3,2,1,0:T(8,128)S(1)} %bitcast.173, bf16[3,2,8,16,1280]{4,3,2,1,0:T(8,128)(2,1)} %bitcast.154), kind=kOutput, calls=%fused_computation.1 | convolution fusion | flops 68714496 | bytes 1835008 | tf_op jit(solution)/shard_map/jbcd,jbch->jbdh/dot_general | solution.py:145
  124.6 2.0 %fusion.1 = bf16[1,1280,768]{2,1,0:T(8,128)(2,1)} fusion(bf16[128,1280]{1,0:T(8,128)(2,1)S(1)} %bitcast.157, bf16[128,768]{1,0:T(8,128)(2,1)S(1)} %copy-done.7, bf16[128,768]{1,0:T(8,128)(2,1)S(1)} %copy-done.5), kind=kOutput, calls=%fused_computation.10 | convolution fusion | flops 253427712 | bytes 2686976 | tf_op jit(solution)/shard_map/dot_general | solution.py:108
  126.5 2.0 %fusion = bf16[1,1280,768]{2,1,0:T(8,128)(2,1)} fusion(bf16[128,1280]{1,0:T(8,128)(2,1)S(1)} %bitcast.158, bf16[128,768]{1,0:T(8,128)(2,1)S(1)} %copy-done.6, bf16[128,768]{1,0:T(8,128)(2,1)S(1)} %copy-done.7, bf16[128,768]{1,0:T(8,128)(2,1)S(1)} %copy-done.5), kind=kOutput, calls=%fused_computation.9 | convolution fusion | flops 253919232 | bytes 2883584 | tf_op jit(solution)/shard_map/dot_general | solution.py:105
  128.5 0.6 fusion.11
  129.2 6.2 %psum.46 = f32[8,1,16]{2,0,1:T(8,128)} all-reduce(f32[8,1,16]{2,0,1:T(8,128)S(1)} %all_to_all.22), channel_id=1, replica_groups=mesh['grp'=4,'ep'=8] {'grp'}, use_global_device_ids=true, to_apply=%region_20.21 | all-reduce | flops 128 | bytes 1024 | tf_op jit(solution)/shard_map/psum | solution.py:155
  135.4 5.5 %all-to-all-start.3 = ((f32[8,1,16]{2,1,0:T(1,128)}), f32[8,1,16]{2,1,0:T(1,128)S(1)}, u32[]{:S(2)}, u32[]{:S(2)}) async-start(f32[8,1,16]{2,1,0:T(1,128)} %bitcast.31), calls=%async_computation.3 | async-start | bytes 8192 | tf_op jit(solution)/shard_map/all_to_all | solution.py:156
  140.9 1.6 fusion.23
  142.6 40.2 %psum.47 = f32[2,8,16]{2,1,0:T(8,128)S(1)} all-reduce(f32[2,8,16]{2,1,0:T(8,128)S(1)} %reshape.204), channel_id=1, replica_groups=mesh['grp'=4,'ep'=8] {'grp','ep'}, use_global_device_ids=true, to_apply=%region_22.23 | all-reduce | flops 256 | bytes 2048 | tf_op jit(solution)/shard_map/psum | solution.py:150
  183.0 2.0 %fusion.2 = bf16[1,768,1280]{2,1,0:T(8,128)(2,1)} fusion(bf16[128,1280]{1,0:T(8,128)(2,1)S(1)} %fusion.37, bf16[128,768]{1,0:T(8,128)(2,1)S(1)} %copy-done.6, bf16[128,768]{1,0:T(8,128)(2,1)S(1)} %copy-done.5), kind=kOutput, calls=%fused_computation.11 | convolution fusion | flops 253427712 | bytes 2686976 | tf_op jit(solution)/shard_map/dot_general | solution.py:111
  185.2 0.5 broadcast.171
  185.7 0.7 reduce.15
  186.4 0.4 convolution_reduce_fusion.1
  187.0 0.7 copy.59
  (68 shorter events, 4.6 us)
Async XLA Ops:
  7.2 61.9 %copy-start = (bf16[1,768,1280]{2,1,0:T(8,128)(2,1)S(1)}, bf16[1,768,1280]{2,1,0:T(8,128)(2,1)}, u32[]{:S(2)}) copy-start(bf16[1,768,1280]{2,1,0:T(8,128)(2,1)} %param.18) | copy-start | bytes 5898244
  7.2 6.9 %copy-start.2 = (bf16[256,1280]{1,0:T(8,128)(2,1)S(1)}, bf16[256,1280]{1,0:T(8,128)(2,1)}, u32[]{:S(2)}) copy-start(bf16[256,1280]{1,0:T(8,128)(2,1)} %param.11) | copy-start | bytes 1966084
  7.2 65.4 %all-gather.3.cloned.1.call-start = ((), (), s32[]{:S(2)}) async-start(), calls=%async_computation.4 | async-start | bytes 2211840 | tf_op jit(solution)/shard_map/all_gather | solution.py:119
  14.4 21.8 %copy-start.3 = (bf16[256,1280]{1,0:T(8,128)(2,1)S(1)}, bf16[256,1280]{1,0:T(8,128)(2,1)}, u32[]{:S(2)}) copy-start(bf16[256,1280]{1,0:T(8,128)(2,1)} %param.12) | copy-start | bytes 1966084
  19.1 13.7 %all-to-all-start.1 = ((bf16[8,1,16]{2,1,0:T(2,128)(2,1)}), bf16[8,1,16]{2,1,0:T(2,128)(2,1)S(1)}, u32[]{:S(2)}, u32[]{:S(2)}) async-start(bf16[8,1,16]{2,1,0:T(2,128)(2,1)} %all_to_all.24), calls=%async_computation.1 | async-start | bytes 8192 | tf_op jit(solution)/shard_map/all_to_all | solution.py:81
  32.8 13.6 %all-to-all-start = ((bf16[8,16,1280]{2,1,0:T(8,128)(2,1)}), bf16[8,16,1280]{2,1,0:T(8,128)(2,1)S(1)}, u32[]{:S(2)}, u32[]{:S(2)}) async-start(bf16[8,16,1280]{2,1,0:T(8,128)(2,1)} %bitcast.165), calls=%async_computation | async-start | bytes 655360 | tf_op jit(solution)/shard_map/all_to_all | solution.py:79
  46.4 22.5 %all-to-all-start.2 = ((bf16[8,16,1280]{2,1,0:T(8,128)(2,1)}), bf16[8,16,1280]{2,1,0:T(8,128)(2,1)S(1)}, u32[]{:S(2)}, u32[]{:S(2)}) async-start(bf16[8,16,1280]{2,1,0:T(8,128)(2,1)} %bitcast.166), calls=%async_computation.2 | async-start | bytes 655360 | tf_op jit(solution)/shard_map/all_to_all | solution.py:80
  50.3 61.4 %all-reduce.3.cloned.1.call-start = ((), (), s32[]{:S(2)}) async-start(), calls=%async_computation.5 | async-start | bytes 1474560 | tf_op jit(solution)/shard_map/psum | solution.py:98
  50.3 2.8 %copy-start.4 = (bf16[1,1280,768]{2,1,0:T(8,128)(2,1)S(1)}, bf16[1,1280,768]{2,1,0:T(8,128)(2,1)}, u32[]{:S(2)}) copy-start(bf16[1,1280,768]{2,1,0:T(8,128)(2,1)} %param.17) | copy-start | bytes 5898244
  74.3 1.5 copy-start.1
  74.3 1.5 copy-start.8
  74.4 1.9 copy-start.9
  75.8 1.1 copy-start.10
  121.1 3.4 %copy-start.5 = (bf16[128,768]{1,0:T(8,128)(2,1)S(1)}, bf16[128,768]{1,0:T(8,128)(2,1)}, u32[]{:S(2)}) copy-start(bf16[128,768]{1,0:T(8,128)(2,1)} %get-tuple-element.36) | copy-start | bytes 589828
  121.1 3.4 %copy-start.7 = (bf16[128,768]{1,0:T(8,128)(2,1)S(1)}, bf16[128,768]{1,0:T(8,128)(2,1)}, u32[]{:S(2)}) copy-start(bf16[128,768]{1,0:T(8,128)(2,1)} %get-tuple-element.35) | copy-start | bytes 589828
  124.5 2.0 %copy-start.6 = (bf16[128,768]{1,0:T(8,128)(2,1)S(1)}, bf16[128,768]{1,0:T(8,128)(2,1)}, u32[]{:S(2)}) copy-start(bf16[128,768]{1,0:T(8,128)(2,1)} %get-tuple-element.34) | copy-start | bytes 589828
  135.4 49.7 %all-to-all-start.3 = ((f32[8,1,16]{2,1,0:T(1,128)}), f32[8,1,16]{2,1,0:T(1,128)S(1)}, u32[]{:S(2)}, u32[]{:S(2)}) async-start(f32[8,1,16]{2,1,0:T(1,128)} %bitcast.31), calls=%async_computation.3 | async-start | bytes 8192 | tf_op jit(solution)/shard_map/all_to_all | solution.py:156
Sparse Core Ops, SparseCore 0:
  15.3 57.2 all-gather.2
  78.1 33.5 all-reduce.2
where the time goes:
time: 195 us
  waiting for transfers between devices  64.2 us (33%)
  blocking collectives  46.4 us (24%)
  matrix products  29.2 us (15%)
  starting transfers between devices  20.2 us (10%)
  between operations  14.4 us (7%)
  local copies, waits for them, and re-layouts  10.9 us (6%)
  other arithmetic  9.22 us (5%)
    psum x1, blocking collectives, body(): hot_route_all = lax.psum(hot_route_part, ('grp', 'ep'))  40.2 us
    psum x1, waiting for transfers between devices, body(): lax.psum(part_up.astype(jnp.bfloat16), 'grp').astype(jnp.float32)  33.6 us
    all_to_all x1, waiting for transfers between devices, body(): lax.all_to_all(outgoing[1], 'ep', split_axis=0, concat_axis=0, tiled=True)  14.6 us
    all_to_all x1, waiting for transfers between devices, body(): lax.all_to_all(outgoing[0], 'ep', split_axis=0, concat_axis=0, tiled=True)  9.11 us
    all_to_all x1, starting transfers between devices, body(): lax.all_to_all(outgoing[2], 'ep', split_axis=0, concat_axis=0, tiled=True)  7.28 us
    psum x1, blocking collectives, body(): cold_route = lax.psum(cold_route, 'grp')  6.24 us
    all_to_all x1, starting transfers between devices, body(): lax.all_to_all(cold_route.reshape(cold_count, capacity), 'ep', split_axis...  5.52 us
    all_to_all x1, waiting for transfers between devices, body(): lax.all_to_all(outgoing[2], 'ep', split_axis=0, concat_axis=0, tiled=True)  4.77 us
  transfers between devices with their start and end apart: 6, of which 5 were waited for; matrix products, arithmetic and copies ran while one was open for 8% of the time, Pallas kernels for 0%

commit v1 on v0

--- a/solution.py
+++ b/solution.py
@@ -147,7 +147,7 @@
     grad_gate_hot = jnp.sum(blk_gate.astype(jnp.bfloat16).astype(jnp.float32), axis=1)
     grad_up_hot = jnp.sum(blk_up.astype(jnp.bfloat16).astype(jnp.float32), axis=1)
     grad_down_hot = jnp.sum(blk_down.astype(jnp.bfloat16).astype(jnp.float32), axis=1)
-    hot_route_all = lax.psum(hot_route_part, ("grp", "ep"))
+    hot_route_all = jnp.sum(lax.all_gather(hot_route_part, axis_name=("grp", "ep")), 0)
     me = lax.axis_index("ep")
     hot_route = lax.dynamic_index_in_dim(
         hot_route_all.reshape(hot_count, blocks, capacity), me, axis=1, keepdims=False

time: 195 us -> 223 us (1.14)
  blocking collectives: 46.4 us -> 73.6 us
    all_gather x0 -> x1, blocking collectives: none -> 67.3 us  [body(): lax.all_gather(hot_route_part, axis_name=('grp', 'ep'))]
    psum x1 -> x0, blocking collectives: 40.2 us -> none  [body(): hot_route_all = lax.psum(hot_route_part, ('grp', 'ep'))]
  transfers between devices with their start and end apart: 6 -> 6, of which waited for: 5 -> 5; matrix products, arithmetic and copies ran while one was open for 8% -> 7% of each run, Pallas kernels for 0% -> 0%
where the time goes in v1:
time: 223 us; the launch traced here: 222 us
  blocking collectives  73.6 us (33%)
  waiting for transfers between devices  64.2 us (29%)
  matrix products  29.2 us (13%)
  starting transfers between devices  20.2 us (9%)
  between operations  14.4 us (6%)
  local copies, waits for them, and re-layouts  10.9 us (5%)
  other arithmetic  9.26 us (4%)
    all_gather x1, blocking collectives, body(): lax.all_gather(hot_route_part, axis_name=('grp', 'ep'))  67.3 us
    psum x1, waiting for transfers between devices, body(): lax.psum(part_up.astype(jnp.bfloat16), 'grp').astype(jnp.float32)  33.6 us
    all_to_all x1, waiting for transfers between devices, body(): lax.all_to_all(outgoing[1], 'ep', split_axis=0, concat_axis=0, tiled=True)  14.6 us
    all_to_all x1, waiting for transfers between devices, body(): lax.all_to_all(outgoing[0], 'ep', split_axis=0, concat_axis=0, tiled=True)  9.11 us
    all_to_all x1, starting transfers between devices, body(): lax.all_to_all(outgoing[2], 'ep', split_axis=0, concat_axis=0, tiled=True)  7.28 us
    psum x1, blocking collectives, body(): cold_route = lax.psum(cold_route, 'grp')  6.24 us
    all_to_all x1, starting transfers between devices, body(): lax.all_to_all(cold_route.reshape(cold_count, capacity), 'ep', split_axis...  5.52 us
    all_to_all x1, waiting for transfers between devices, body(): lax.all_to_all(outgoing[2], 'ep', split_axis=0, concat_axis=0, tiled=True)  4.77 us
  transfers between devices with their start and end apart: 6, of which 5 were waited for; matrix products, arithmetic and copies ran while one was open for 7% of the time, Pallas kernels for 0%

profile of v1, /device:TPU:0, one launch (start us, length us, event | category | flops | bytes accessed | tf_op | source)
XLA Modules:
  0.0 221.7 jit_solution(12911008587821388085)
XLA Ops:
  7.2 1.0 copy.45
  8.5 0.8 copy.49
  9.5 0.7 compare_convert_fusion.1
  10.2 0.6 reduce-window.16
  11.2 0.8 fusion.78
  12.8 1.3 convolution_convert_fusion.8
  14.4 0.7 pad_maximum_fusion
  15.2 2.3 %reduce-window.14 = s32[8,12,128]{2,1,0:T(8,128)S(1)} reduce-window(s32[8,12,128]{2,1,0:T(8,128)S(1)} %fusion.69, s32[]{:T(128)} %constant.15.clone.1), window={size=1x1x128 pad=0_0x0_0x127_0}, to_apply=%region_1.2 | reduce-window | flops 1560576 | bytes 98308 | tf_op jit(solution)/shard_map/reduce-window
  17.5 0.3 slice_reduce_fusion
  18.4 0.7 all_to_all.24
  19.1 7.3 %all-to-all-start.1 = ((bf16[8,1,16]{2,1,0:T(2,128)(2,1)}), bf16[8,1,16]{2,1,0:T(2,128)(2,1)S(1)}, u32[]{:S(2)}, u32[]{:S(2)}) async-start(bf16[8,1,16]{2,1,0:T(2,128)(2,1)} %all_to_all.24), calls=%async_computation.1 | async-start | bytes 8192 | tf_op jit(solution)/shard_map/all_to_all | solution.py:81
  27.0 1.0 convolution_convert_fusion.7
  28.0 4.8 %all-to-all-done.1 = bf16[8,1,16]{2,1,0:T(2,128)(2,1)S(1)} async-done(((bf16[8,1,16]{2,1,0:T(2,128)(2,1)}), bf16[8,1,16]{2,1,0:T(2,128)(2,1)S(1)}, u32[]{:S(2)}, u32[]{:S(2)}) %all-to-all-start.1) | async-done | bytes 288 | tf_op jit(solution)/shard_map/all_to_all | solution.py:81
  32.8 3.4 %all-to-all-start = ((bf16[8,16,1280]{2,1,0:T(8,128)(2,1)}), bf16[8,16,1280]{2,1,0:T(8,128)(2,1)S(1)}, u32[]{:S(2)}, u32[]{:S(2)}) async-start(bf16[8,16,1280]{2,1,0:T(8,128)(2,1)} %bitcast.166), calls=%async_computation | async-start | bytes 655360 | tf_op jit(solution)/shard_map/all_to_all | solution.py:79
  36.2 1.0 convolution_convert_fusion.6
  37.3 9.1 %all-to-all-done = bf16[8,16,1280]{2,1,0:T(8,128)(2,1)S(1)} async-done(((bf16[8,16,1280]{2,1,0:T(8,128)(2,1)}), bf16[8,16,1280]{2,1,0:T(8,128)(2,1)S(1)}, u32[]{:S(2)}, u32[]{:S(2)}) %all-to-all-start) | async-done | bytes 327712 | tf_op jit(solution)/shard_map/all_to_all | solution.py:79
  46.4 3.9 %all-to-all-start.2 = ((bf16[8,16,1280]{2,1,0:T(8,128)(2,1)}), bf16[8,16,1280]{2,1,0:T(8,128)(2,1)S(1)}, u32[]{:S(2)}, u32[]{:S(2)}) async-start(bf16[8,16,1280]{2,1,0:T(8,128)(2,1)} %bitcast.167), calls=%async_computation.2 | async-start | bytes 655360 | tf_op jit(solution)/shard_map/all_to_all | solution.py:80
  50.3 2.8 %fusion.20 = bf16[128,768]{1,0:T(8,128)(2,1)} fusion(bf16[128,1280]{1,0:T(8,128)(2,1)S(1)} %bitcast.156, bf16[1,1280,768]{2,1,0:T(8,128)(2,1)} %param.16), kind=kOutput, calls=%fused_computation.29 | convolution fusion | flops 251756544 | bytes 2490368 | tf_op jit(solution)/shard_map/dot_general | solution.py:91
  53.1 1.1 fusion.17
  54.3 14.6 %all-to-all-done.2 = bf16[8,16,1280]{2,1,0:T(8,128)(2,1)S(1)} async-done(((bf16[8,16,1280]{2,1,0:T(8,128)(2,1)}), bf16[8,16,1280]{2,1,0:T(8,128)(2,1)S(1)}, u32[]{:S(2)}, u32[]{:S(2)}) %all-to-all-start.2) | async-done | bytes 327712 | tf_op jit(solution)/shard_map/all_to_all | solution.py:80
  69.0 1.5 fusion.14
  70.5 2.1 all-gather.5.cloned.1.call-done
  72.6 1.7 copy.68
  74.4 1.0 fusion.92
  75.3 0.5 copy-done.1
  75.8 0.3 fusion.25
  76.3 0.3 fusion.24
  76.6 0.3 copy-done.10
  76.9 0.3 fusion.26
  77.2 0.7 pad_maximum_fusion.1
  78.1 33.6 %all-reduce.3.cloned.1.call-done = (bf16[128,768]{1,0:T(8,128)(2,1)}, bf16[128,768]{1,0:T(8,128)(2,1)}, bf16[128,768]{1,0:T(8,128)(2,1)}, bf16[3,2,128,96]{2,3,1,0:T(8,128)(2,1)}) async-done(((bf16[128,768]{1,0:T(8,128)(2,1)}, bf16[128,768]{1,0:T(8,128)(2,1)}, bf16[128,768]{1,0:T(8,128)(2,1)}, bf16[3,2,128,96]{2,3,1,0:T(8,128)(2,1)}), (bf16[128,768]{1,0:T(8,128)(2,1)}, bf16[128,768]{1,0:T(8,128)(2,1)}, ...) | async-done | bytes 737296 | tf_op jit(solution)/shard_map/psum | solution.py:98
  111.7 1.6 convert_element_type.217
  113.3 0.9 fusion.93
  114.5 3.3 %convert_reduce_fusion = f32[2,96,1280]{2,1,0:T(8,128)} fusion(f32[2,8,16,96]{3,2,1,0:T(8,128)S(1)} %bitcast.170, f32[2,8,16,96]{3,2,1,0:T(8,128)S(1)} %bitcast.172, bf16[3,2,8,16,1280]{4,3,2,1,0:T(8,128)(2,1)} %bitcast.153), kind=kOutput, calls=%fused_computation | convolution fusion | flops 68714496 | bytes 1835008 | tf_op jit(solution)/shard_map/jbch,jbcd->jbhd/dot_general | solution.py:146
  117.8 3.3 %convert_reduce_fusion.2 = f32[2,1280,96]{1,2,0:T(8,128)} fusion(f32[2,8,16,96]{3,2,1,0:T(8,128)S(1)} %bitcast.173, f32[2,8,16,96]{3,2,1,0:T(8,128)S(1)} %bitcast.175, f32[2,8,16,96]{3,2,1,0:T(8,128)S(1)} %bitcast.171, bf16[3,2,8,16,1280]{4,3,2,1,0:T(8,128)(2,1)} %bitcast.154), kind=kOutput, calls=%fused_computation.2 | convolution fusion | flops 68812800 | bytes 1933312 | tf_op jit(solution)/shard_map/jbcd,jbch->jbdh/dot_general | solution.py:144
  121.1 3.4 %convert_reduce_fusion.1 = f32[2,1280,96]{1,2,0:T(8,128)} fusion(f32[2,8,16,96]{3,2,1,0:T(8,128)S(1)} %bitcast.176, f32[2,8,16,96]{3,2,1,0:T(8,128)S(1)} %bitcast.174, bf16[3,2,8,16,1280]{4,3,2,1,0:T(8,128)(2,1)} %bitcast.155), kind=kOutput, calls=%fused_computation.1 | convolution fusion | flops 68714496 | bytes 1835008 | tf_op jit(solution)/shard_map/jbcd,jbch->jbdh/dot_general | solution.py:145
  124.6 2.0 fusion.1
  126.5 2.0 fusion
  128.5 0.6 fusion.11
  129.2 6.2 %psum.39 = f32[8,1,16]{2,0,1:T(8,128)} all-reduce(f32[8,1,16]{2,0,1:T(8,128)S(1)} %all_to_all.22), channel_id=1, replica_groups=mesh['grp'=4,'ep'=8] {'grp'}, use_global_device_ids=true, to_apply=%region_20.21 | all-reduce | flops 128 | bytes 1024 | tf_op jit(solution)/shard_map/psum | solution.py:155
  135.4 5.5 %all-to-all-start.3 = ((f32[8,1,16]{2,1,0:T(1,128)}), f32[8,1,16]{2,1,0:T(1,128)S(1)}, u32[]{:S(2)}, u32[]{:S(2)}) async-start(f32[8,1,16]{2,1,0:T(1,128)} %bitcast.31), calls=%async_computation.3 | async-start | bytes 8192 | tf_op jit(solution)/shard_map/all_to_all | solution.py:156
  140.9 1.6 fusion.23
  142.6 67.3 %all-gather.2 = f32[32,2,128]{2,1,0:T(2,128)S(1)} all-gather(f32[1,2,128]{2,1,0:T(2,128)S(1)} %bitcast.179), channel_id=3, replica_groups=mesh['grp'=4,'ep'=8] {'grp','ep'}, dimensions={0}, use_global_device_ids=true | all-gather | bytes 33792 | tf_op jit(solution)/shard_map/all_gather | solution.py:150
  210.1 2.0 fusion.2
  212.4 0.5 broadcast.171
  212.9 0.7 reduce.16
  213.6 0.4 convolution_reduce_fusion.1
  214.2 0.7 copy.59
  (69 shorter events, 4.7 us)
Async XLA Ops:
  7.2 61.9 %copy-start = (bf16[1,768,1280]{2,1,0:T(8,128)(2,1)S(1)}, bf16[1,768,1280]{2,1,0:T(8,128)(2,1)}, u32[]{:S(2)}) copy-start(bf16[1,768,1280]{2,1,0:T(8,128)(2,1)} %param.18) | copy-start | bytes 5898244
  7.2 6.9 %copy-start.2 = (bf16[256,1280]{1,0:T(8,128)(2,1)S(1)}, bf16[256,1280]{1,0:T(8,128)(2,1)}, u32[]{:S(2)}) copy-start(bf16[256,1280]{1,0:T(8,128)(2,1)} %param.11) | copy-start | bytes 1966084
  7.2 65.4 %all-gather.5.cloned.1.call-start = ((), (), s32[]{:S(2)}) async-start(), calls=%async_computation.4 | async-start | bytes 2211840 | tf_op jit(solution)/shard_map/all_gather | solution.py:119
  14.4 21.8 %copy-start.3 = (bf16[256,1280]{1,0:T(8,128)(2,1)S(1)}, bf16[256,1280]{1,0:T(8,128)(2,1)}, u32[]{:S(2)}) copy-start(bf16[256,1280]{1,0:T(8,128)(2,1)} %param.12) | copy-start | bytes 1966084
  19.1 13.7 %all-to-all-start.1 = ((bf16[8,1,16]{2,1,0:T(2,128)(2,1)}), bf16[8,1,16]{2,1,0:T(2,128)(2,1)S(1)}, u32[]{:S(2)}, u32[]{:S(2)}) async-start(bf16[8,1,16]{2,1,0:T(2,128)(2,1)} %all_to_all.24), calls=%async_computation.1 | async-start | bytes 8192 | tf_op jit(solution)/shard_map/all_to_all | solution.py:81
  32.8 13.6 %all-to-all-start = ((bf16[8,16,1280]{2,1,0:T(8,128)(2,1)}), bf16[8,16,1280]{2,1,0:T(8,128)(2,1)S(1)}, u32[]{:S(2)}, u32[]{:S(2)}) async-start(bf16[8,16,1280]{2,1,0:T(8,128)(2,1)} %bitcast.166), calls=%async_computation | async-start | bytes 655360 | tf_op jit(solution)/shard_map/all_to_all | solution.py:79
  46.4 22.5 %all-to-all-start.2 = ((bf16[8,16,1280]{2,1,0:T(8,128)(2,1)}), bf16[8,16,1280]{2,1,0:T(8,128)(2,1)S(1)}, u32[]{:S(2)}, u32[]{:S(2)}) async-start(bf16[8,16,1280]{2,1,0:T(8,128)(2,1)} %bitcast.167), calls=%async_computation.2 | async-start | bytes 655360 | tf_op jit(solution)/shard_map/all_to_all | solution.py:80
  50.3 61.4 %all-reduce.3.cloned.1.call-start = ((), (), s32[]{:S(2)}) async-start(), calls=%async_computation.5 | async-start | bytes 1474560 | tf_op jit(solution)/shard_map/psum | solution.py:98
  50.3 2.8 %copy-start.4 = (bf16[1,1280,768]{2,1,0:T(8,128)(2,1)S(1)}, bf16[1,1280,768]{2,1,0:T(8,128)(2,1)}, u32[]{:S(2)}) copy-start(bf16[1,1280,768]{2,1,0:T(8,128)(2,1)} %param.17) | copy-start | bytes 5898244
  74.3 1.5 copy-start.1
  74.3 1.5 copy-start.8
  74.4 1.9 copy-start.9
  75.8 1.1 copy-start.10
  121.1 3.4 %copy-start.5 = (bf16[128,768]{1,0:T(8,128)(2,1)S(1)}, bf16[128,768]{1,0:T(8,128)(2,1)}, u32[]{:S(2)}) copy-start(bf16[128,768]{1,0:T(8,128)(2,1)} %get-tuple-element.36) | copy-start | bytes 589828
  121.1 3.4 %copy-start.7 = (bf16[128,768]{1,0:T(8,128)(2,1)S(1)}, bf16[128,768]{1,0:T(8,128)(2,1)}, u32[]{:S(2)}) copy-start(bf16[128,768]{1,0:T(8,128)(2,1)} %get-tuple-element.35) | copy-start | bytes 589828
  124.5 2.0 copy-start.6
  135.4 76.9 %all-to-all-start.3 = ((f32[8,1,16]{2,1,0:T(1,128)}), f32[8,1,16]{2,1,0:T(1,128)S(1)}, u32[]{:S(2)}, u32[]{:S(2)}) async-start(f32[8,1,16]{2,1,0:T(1,128)} %bitcast.31), calls=%async_computation.3 | async-start | bytes 8192 | tf_op jit(solution)/shard_map/all_to_all | solution.py:156
Sparse Core Ops, SparseCore 0:
  15.3 57.2 all-gather.4
  78.1 33.5 all-reduce.2
